TPU v7x, 256 devices: a whole 4x4x8 slice. The times are simulated.
256 devices in a mesh: people: 2 (over x_hi), tm: 64 (over z, y, core), type: 2 (over x_lo).
Axes of the slice: x: 4 (x_hi: 2, x_lo: 2; x = x_hi * 2 + x_lo), y: 4, z: 8, core: 2. Of those that a mesh axis runs over, the one named last changes fastest.
Arguments:
- features: bfloat16 [3, 2, 16384], P(None, 'people', 'tm'), may hold values from -6 to 6
- wear: int32 [2, 16384], P('people', 'tm'), may hold values 0 or 1
- rec_start: int32 [2], P('people'), may hold values from 0 to 255
- rec_end: int32 [2], P('people'), may hold values from 16129 to 16384
- conv_first: bfloat16 [3, 3, 128], replicated, may hold values from -2 to 2
- conv_second: bfloat16 [3, 128, 128], replicated, may hold values from -0.3125 to 0.3125
- emit_weight: bfloat16 [128, 512], P(None, 'type'), may hold values from -0.5 to 0.5
- leave: float32 [8, 64], P('type'), may hold values from 0.002 to 0.5
- jump: float32 [8, 64, 64], P('type'), may hold values from -6 to 6
- init_logits: float32 [8, 64], P('type'), may hold values from -6 to 6
- type_prior: float32 [8], replicated, may hold values from -4 to 4
Outputs:
- loglik_rate: float32 [2, 8], P('people', 'type')
- type_post: float32 [2, 8], P('people', 'type')
- occupancy: float32 [8, 64], P('type')
- filtered: float32 [2, 16384, 8, 64], P('people', 'tm', 'type')
All inputs are finite; a program needn't handle non-finite values. No bound on the sum of `wear` on one device may be relied on, other than what follows from the above.
Results may differ from a plain program's by a relative error of at most 0.0085.
Values may be sent and summed in bfloat16 or wider, within the bound.
No kernel may reach another device: no remote copies, remote signals or barrier semaphores. Data moves between devices by JAX's collectives and lax.ppermute only.
A program may use at most 64 MiB of HBM per device.

v0:
```python
import jax
import jax.numpy as jnp
from jax import lax
from jax.sharding import PartitionSpec as P

HIGH = lax.Precision.HIGHEST


def padded(block, sides, width):
    for axis, dim in sides:
        count = lax.axis_size(axis)
        forward = [(i, i + 1) for i in range(count - 1)]
        backward = [(target, source) for source, target in forward]
        low = lax.ppermute(
            lax.slice_in_dim(block, block.shape[dim] - width, None, axis=dim), axis, forward
        )
        high = lax.ppermute(lax.slice_in_dim(block, 0, width, axis=dim), axis, backward)
        block = jnp.concatenate([low, block, high], axis=dim)
    return block


def prefix(shard, axis, combine, identity):
    size, mine = (lax.axis_size(axis), lax.axis_index(axis))
    everything = jax.tree.map(
        lambda part, kind: lax.all_gather(part.astype(kind), axis),
        shard,
        (jnp.bfloat16, jnp.bfloat16),
    )
    start = jax.tree.map(
        lambda part, zero: jnp.broadcast_to(jnp.asarray(zero, part.dtype), part.shape),
        shard,
        identity,
    )

    def turn(k, before):
        reached = k < mine
        new = combine(
            before, jax.tree.map(lambda part, own: part[k].astype(own.dtype), everything, shard)
        )
        return jax.tree.map(lambda a, b: jnp.where(reached, a, b), new, before)

    return lax.fori_loop(0, size, turn, start)


def chain_join(earlier, later):
    left, left_log = earlier
    right, right_log = later
    joined = jnp.einsum("...ij,...jk->...ik", left, right, precision=HIGH)
    scale = jnp.sum(joined, axis=(-2, -1)) / joined.shape[-1]
    return (joined / scale[..., None, None], left_log + right_log + jnp.log(scale))


def chain_product(mats, logs):
    while mats.shape[0] > 1:
        half = mats.shape[0] // 2
        joined, joined_log = chain_join(
            (mats[0 : 2 * half : 2], logs[0 : 2 * half : 2]),
            (mats[1 : 2 * half : 2], logs[1 : 2 * half : 2]),
        )
        mats, logs = (joined, joined_log)
    return (mats[0], logs[0])


def on_device(
    features,
    wear,
    rec_start,
    rec_end,
    conv_first,
    conv_second,
    emit_weight,
    leave,
    jump,
    init_logits,
    type_prior,
):
    persons = features.shape[1]
    span = features.shape[2]
    kinds = jump.shape[0]
    states = jump.shape[-1]
    tm_index = lax.axis_index("tm")
    type_index = lax.axis_index("type")
    total_epochs = span * lax.axis_size("tm")
    extended = padded(features, (("tm", 2),), 5)
    first = jnp.zeros((persons, span + 8, conv_first.shape[2]), jnp.float32)
    for tap in range(3):
        first = first + jnp.einsum(
            "ipt,ic->ptc",
            extended[:, :, tap : tap + span + 8],
            conv_first[tap],
            preferred_element_type=jnp.float32,
        )
    wide_pos = tm_index * span - 4 + jnp.arange(span + 8, dtype=jnp.int32)
    inside = (wide_pos >= 0) & (wide_pos < total_epochs)
    first = jnp.where(inside[None, :, None], jax.nn.silu(first), 0.0).astype(jnp.bfloat16)
    second = jnp.zeros((persons, span, conv_second.shape[2]), jnp.float32)
    for tap in range(3):
        second = second + jnp.einsum(
            "ptc,cd->ptd",
            first[:, 4 * tap : 4 * tap + span],
            conv_second[tap],
            preferred_element_type=jnp.float32,
        )
    second = jax.nn.silu(second).astype(jnp.bfloat16)
    logits = jnp.einsum("ptc,cm->ptm", second, emit_weight, preferred_element_type=jnp.float32)
    probs = jnp.exp(jax.nn.log_softmax(logits.reshape(persons, span, kinds, states), axis=-1))
    positions = tm_index * span + jnp.arange(span, dtype=jnp.int32)
    observed = (
        (wear > 0)
        & (positions[None, :] >= rec_start[:, None])
        & (positions[None, :] < rec_end[:, None])
    )
    emis = jnp.where(observed[:, :, None, None], probs, jnp.float32(1.0))
    observed_f = observed.astype(jnp.float32)
    eye_small = jnp.eye(states, dtype=jnp.float32)
    trans = (1.0 - leave)[..., None] * eye_small + leave[..., None] * jax.nn.softmax(jump, axis=-1)
    start = jax.nn.softmax(init_logits, axis=-1)
    start_all = jnp.broadcast_to(start, (persons, kinds, states))
    group = span // 16
    emis_blocks = jnp.transpose(emis.reshape(persons, 16, group, kinds, states), (1, 2, 0, 3, 4))
    eye_all = jnp.broadcast_to(eye_small, (persons, kinds, states, states))
    zero_logs = jnp.zeros((persons, kinds), jnp.float32)

    def block_leaves(block):
        return trans[None, None] * block[..., None, :]

    def pass_one(carry, block):
        leaves = block_leaves(block)
        product = chain_product(leaves, jnp.zeros(leaves.shape[:3], jnp.float32))
        return (chain_join(carry, product), None)

    (stretch, stretch_log), _ = lax.scan(pass_one, (eye_all, zero_logs), emis_blocks)
    before, before_log = prefix((stretch, stretch_log), "tm", chain_join, (eye_all, zero_logs))
    vec = jnp.einsum("pki,pkij->pkj", start_all, before, precision=HIGH)
    vec_total = jnp.sum(vec, axis=-1)
    alpha_in = vec / vec_total[..., None]
    log_in = before_log + jnp.log(vec_total)

    def advance(carry, inputs):
        alpha_now, log_now, occupied = carry
        emis_now, mask_now = inputs
        pred = jnp.einsum("pki,kij->pkj", alpha_now, trans, precision=HIGH)
        unnorm = pred * emis_now
        step_total = jnp.sum(unnorm, axis=-1)
        alpha_next = unnorm / step_total[..., None]
        occupied = occupied + mask_now[:, None, None] * alpha_next
        return ((alpha_next, log_now + jnp.log(step_total), occupied), alpha_next)

    zero_occupied = jnp.zeros((persons, kinds, states), jnp.float32)
    (alpha_end, own_log, occupied), history = lax.scan(
        advance,
        (alpha_in, zero_logs, zero_occupied),
        (jnp.transpose(emis, (1, 0, 2, 3)), observed_f.T),
    )
    filtered = jnp.transpose(history, (1, 0, 2, 3))
    contribution = log_in + own_log - log_in
    summed = lax.psum(contribution, "tm")
    full = lax.all_gather(summed, "type", axis=1, tiled=True)
    rate_full = full / total_epochs
    post_full = jax.nn.softmax(type_prior[None, :] + 8.0 * rate_full, axis=-1)
    offset = type_index * kinds
    rate_own = lax.dynamic_slice(rate_full, (jnp.int32(0), offset), (persons, kinds))
    post_own = lax.dynamic_slice(post_full, (jnp.int32(0), offset), (persons, kinds))
    numer = jnp.einsum("pk,pks->ks", post_own, occupied, precision=HIGH)
    denom = jnp.einsum("pk,p->k", post_own, jnp.sum(observed_f, axis=1), precision=HIGH)
    numer, denom = lax.psum((numer, denom), ("people", "tm"))
    occupancy = numer / denom[:, None]
    return (rate_own, post_own, occupancy, filtered)


def solution(mesh):
    return jax.shard_map(
        on_device,
        mesh=mesh,
        in_specs=(
            P(None, "people", "tm"),
            P("people", "tm"),
            P("people"),
            P("people"),
            P(),
            P(),
            P(None, "type"),
            P("type", None),
            P("type", None, None),
            P("type", None),
            P(),
        ),
        out_specs=(
            P("people", "type"),
            P("people", "type"),
            P("type", None),
            P("people", "tm", "type", None),
        ),
        check_vma=False,
    )
```

profile of v0, /device:TPU:1, one launch (start us, length us, event | category | flops | bytes accessed | tf_op | source)
XLA Modules:
  0.0 1187.6 jit_solution(14869745420775426021)
XLA Ops:
  8.0 4.6 collective-permute-start
  12.6 1.9 collective-permute-start.1
  15.9 1.3 convert_reduce_fusion
  18.1 1.5 fusion.37
  26.5 85.7 %while.46 = (s32[]{:T(128)}, f32[1,4,64,64]{2,3,1,0:T(8,128)S(1)}, f32[1,4]{1,0:T(1,128)S(1)}, f32[4,64,64]{2,1,0:T(8,128)S(1)}, f32[16,16,1,4,64]{4,3,1,2,0:T(4,128)S(1)}, /*index=5*/s32[]{:T(128)}, s32[]{:T(128)}) while((s32[]{:T(128)}, f32[1,4,64,64]{2,3,1,0:T(8,128)S(1)}, f32[1,4]{1,0:T(1,128)S(1)}, ...), condition=%wide.region_10.11_spmd.clone, body=%wide.region_4.0_spmd.clone.sunk | while | flops 202113104 | bytes 6277803 | solution.py:132
  26.8 1.4 fusion.97
  32.2 1.4 fusion.97
  37.5 1.4 fusion.97
  42.9 1.4 fusion.97
  48.3 1.4 fusion.97
  53.6 1.4 fusion.97
  59.0 1.4 fusion.97
  64.3 1.4 fusion.97
  69.7 1.4 fusion.97
  75.0 1.4 fusion.97
  80.4 1.4 fusion.97
  85.8 1.4 fusion.97
  91.1 1.4 fusion.97
  96.5 1.4 fusion.97
  101.8 1.4 fusion.97
  107.2 1.4 fusion.97
  115.0 43.8 %all-gather.2 = bf16[64,1,4]{2,1,0:T(2,128)(2,1)S(1)} all-gather(bf16[1,1,4]{2,1,0:T(2,128)(2,1)S(1)} %convert_bitcast_fusion.1), channel_id=3, replica_groups=mesh['people'=2,'tm'=64,'type'=2] {'tm'}, dimensions={0}, use_global_device_ids=true | all-gather | bytes 520 | tf_op jit(solution)/shard_map/all_gather | solution.py:25
  158.7 1.6 exponential_select_fusion
  160.4 36.0 %all-gather.5.cloned.1.call-done = bf16[64,4,64,64]{3,2,1,0:T(8,128)(2,1)} async-done(((bf16[1,4,64,64]{3,2,1,0:T(8,128)(2,1)}), bf16[64,4,64,64]{3,2,1,0:T(8,128)(2,1)}) %all-gather.5.cloned.1.call-update) | async-done | bytes 2097168 | tf_op jit(solution)/shard_map/all_gather | solution.py:25
  196.4 86.0 %while.47 = (s32[]{:T(128)}, f32[1,4,64,64]{2,3,1,0:T(8,128)S(1)}, f32[1,4]{1,0:T(1,128)S(1)}, s32[]{:T(128)}, bf16[64,1,4,64,64]{4,3,2,0,1:T(8,128)(2,1)}, /*in...) while((s32[]{:T(128)}, f32[1,4,64,64]{2,3,1,0:T(8,128)S(1)}, f32[1,4]{1,0:T(1,128)S(1)}, ...), condition=%wide.region_13.14_spmd.clone, body=%wide.region_11.13_spmd.clone.sunk | while | flops 12632092 | bytes 393958 | solution.py:42
  199.1 1.2 fusion.104
  205.8 1.2 fusion.104
  282.9 438.0 %while.48 = (s32[]{:T(128)}, f32[1,4,64]{2,1,0:T(4,128)S(1)}, f32[1,4]{1,0:T(1,128)S(1)}, f32[1,4,64]{2,1,0:T(4,128)S(1)}, f32[256,1,4,64]{3,2,1,0:T(4,128)S(1)}...) while((s32[]{:T(128)}, f32[1,4,64]{2,1,0:T(4,128)S(1)}, ...), condition=%wide.region_19.20_spmd.clone, body=%wide.region_17.19_spmd.clone.sunk | while | flops 198407 | bytes 81608 | solution.py:150
  721.0 123.7 %psum.21 = f32[1,4]{1,0:T(1,128)S(1)} all-reduce(f32[1,4]{1,0:T(1,128)S(1)} %add_subtract_fusion), channel_id=1, replica_groups=mesh['people'=2,'tm'=64,'type'=2] {'tm'}, use_global_device_ids=true, to_apply=%region_20.21 | all-reduce | flops 4 | bytes 32 | tf_op jit(solution)/shard_map/psum | solution.py:157
  845.7 3.8 all-reduce
  850.0 1.3 fusion.68
  853.3 326.8 %all-reduce.1 = (f32[4,64]{1,0:T(4,128)S(1)}, f32[4]{0:T(128)S(1)}) all-reduce(f32[4,64]{1,0:T(4,128)S(1)} %bitcast_multiply_fusion.1, f32[4]{0:T(128)S(1)} %get-tuple-element.317), channel_id=1, replica_groups=mesh['people'=2,'tm'=64,'type'=2] {'people','tm'}, use_global_device_ids=true, to_apply=%region_23.24 | all-reduce | flops 260 | bytes 2080 | tf_op jit(solution)/shard_map/psum | solution.py:166
  (2286 shorter events, 591.4 us)
Async XLA Ops:
  7.2 17.2 %copy-start = (bf16[128,256]{1,0:T(8,128)(2,1)S(1)}, bf16[128,256]{1,0:T(8,128)(2,1)}, u32[]{:S(2)}) copy-start(bf16[128,256]{1,0:T(8,128)(2,1)} %param.23) | copy-start | bytes 196612
  7.2 17.0 %copy-start.1 = (bf16[3,128,128]{2,1,0:T(8,128)(2,1)S(1)}, bf16[3,128,128]{2,1,0:T(8,128)(2,1)}, u32[]{:S(2)}) copy-start(bf16[3,128,128]{2,1,0:T(8,128)(2,1)} %param.22) | copy-start | bytes 294916
  7.2 189.2 %all-gather.5.cloned.1.call-start = ((), (), s32[]{:S(2)}) async-start(), calls=%async_computation | async-start | bytes 4259840 | tf_op jit(solution)/shard_map/all_gather | solution.py:25
  8.0 11.6 collective-permute-start
  12.6 7.0 collective-permute-start.1
  26.5 86.6 %copy-start.2 = (f32[4,64]{1,0:T(4,128)S(1)}, f32[4,64]{1,0:T(4,128)}, u32[]{:S(2)}) copy-start(f32[4,64]{1,0:T(4,128)} %param.26) | copy-start | bytes 3076
  26.5 86.7 %copy-start.5 = (u32[256]{0:T(256)S(1)}, u32[256]{0:T(256)}, u32[]{:S(2)}) copy-start(u32[256]{0:T(256)} %constant.125) | copy-start | bytes 3076
  196.4 653.0 %copy-start.4 = (f32[8]{0:T(128)S(1)}, f32[8]{0:T(128)}, u32[]{:S(2)}) copy-start(f32[8]{0:T(128)} %param.27) | copy-start | bytes 100
  853.2 327.5 %copy-start.3 = (f32[1,4]{1,0:T(1,128)}, f32[1,4]{1,0:T(1,128)S(1)}, u32[]{:S(2)}) copy-start(f32[1,4]{1,0:T(1,128)S(1)} %get-tuple-element.318) | copy-start | bytes 52
Sparse Core Ops, SparseCore 0:
  113.1 83.2 all-gather.4
where the time goes:
time: 1190 us
  blocking collectives  498 us (42%)
  other arithmetic  258 us (22%)
  matrix products  195 us (16%)
  local copies, waits for them, and re-layouts  168 us (14%)
  waiting for transfers between devices  36 us (3%)
  between operations  16.3 us (1%)
    psum x1, blocking collectives, on_device(): numer, denom = lax.psum((numer, denom), ('people', 'tm'))  327 us
    add x256, other arithmetic, advance(): occupied = occupied + mask_now[:, None, None] * alpha_next  168 us
    dynamic_slice x256, local copies, waits for them, and re-layouts, on_device(): lax.scan(advance, (alpha_in, zero_logs, zero_occupied), (jnp.transpose(em...  151 us
    dot_general x144, matrix products, chain_join(): joined = jnp.einsum('...ij,...jk->...ik', left, right, precision=HIGH)  134 us
    psum x1, blocking collectives, on_device(): summed = lax.psum(contribution, 'tm')  124 us
    dot_general x256, matrix products, advance(): pred = jnp.einsum('pki,kij->pkj', alpha_now, trans, precision=HIGH)  57.1 us
    all_gather x1, blocking collectives, prefix(): lax.all_gather(part.astype(kind), axis)  43.8 us
    all_gather x1, waiting for transfers between devices, prefix(): lax.all_gather(part.astype(kind), axis)  36 us
  transfers between devices with their start and end apart: 3, of which 1 were waited for; matrix products, arithmetic and copies ran while one was open for 1% of the time, Pallas kernels for 0%

commit v1 on v0

--- a/solution.py
+++ b/solution.py
@@ -154,7 +154,7 @@
     )
     filtered = jnp.transpose(history, (1, 0, 2, 3))
     contribution = log_in + own_log - log_in
-    summed = lax.psum(contribution, "tm")
+    summed = jnp.sum(lax.all_gather(contribution, "tm"), axis=0)
     full = lax.all_gather(summed, "type", axis=1, tiled=True)
     rate_full = full / total_epochs
     post_full = jax.nn.softmax(type_prior[None, :] + 8.0 * rate_full, axis=-1)

time: 1190 us -> 1110 us (0.933)
  blocking collectives: 498 us -> 409 us
    psum x1 -> x0, blocking collectives: 124 us -> none  [on_device(): summed = lax.psum(contribution, 'tm')]
    all_gather x0 -> x1, blocking collectives: none -> 37.5 us  [on_device(): summed = jnp.sum(lax.all_gather(contribution, 'tm'), axis=0)]
where the time goes in v1:
time: 1110 us; the launch traced here: 1100 us
  blocking collectives  409 us (37%)
  other arithmetic  258 us (23%)
  matrix products  195 us (18%)
  local copies, waits for them, and re-layouts  168 us (15%)
  waiting for transfers between devices  36 us (3%)
  between operations  16.3 us (1%)
    psum x1, blocking collectives, on_device(): numer, denom = lax.psum((numer, denom), ('people', 'tm'))  324 us
    add x256, other arithmetic, advance(): occupied = occupied + mask_now[:, None, None] * alpha_next  168 us
    dynamic_slice x256, local copies, waits for them, and re-layouts, on_device(): lax.scan(advance, (alpha_in, zero_logs, zero_occupied), (jnp.transpose(em...  151 us
    dot_general x144, matrix products, chain_join(): joined = jnp.einsum('...ij,...jk->...ik', left, right, precision=HIGH)  134 us
    dot_general x256, matrix products, advance(): pred = jnp.einsum('pki,kij->pkj', alpha_now, trans, precision=HIGH)  57.1 us
    all_gather x1, blocking collectives, prefix(): lax.all_gather(part.astype(kind), axis)  43.8 us
    all_gather x1, blocking collectives, on_device(): summed = jnp.sum(lax.all_gather(contribution, 'tm'), axis=0)  37.5 us
    all_gather x1, waiting for transfers between devices, prefix(): lax.all_gather(part.astype(kind), axis)  36 us
  transfers between devices with their start and end apart: 3, of which 1 were waited for; matrix products, arithmetic and copies ran while one was open for 1% of the time, Pallas kernels for 0%

profile of v1, /device:TPU:1, one launch (start us, length us, event | category | flops | bytes accessed | tf_op | source)
XLA Modules:
  0.0 1099.2 jit_solution(9225135185024129812)
XLA Ops:
  8.0 4.6 collective-permute-start
  12.6 1.9 collective-permute-start.1
  15.9 1.3 convert_reduce_fusion
  18.1 1.5 fusion.37
  26.5 85.7 %while.46 = (s32[]{:T(128)}, f32[1,4,64,64]{2,3,1,0:T(8,128)S(1)}, f32[1,4]{1,0:T(1,128)S(1)}, f32[4,64,64]{2,1,0:T(8,128)S(1)}, f32[16,16,1,4,64]{4,3,1,2,0:T(4,128)S(1)}, /*index=5*/s32[]{:T(128)}, s32[]{:T(128)}) while((s32[]{:T(128)}, f32[1,4,64,64]{2,3,1,0:T(8,128)S(1)}, f32[1,4]{1,0:T(1,128)S(1)}, ...), condition=%wide.region_10.11_spmd.clone, body=%wide.region_4.0_spmd.clone.sunk | while | flops 202113104 | bytes 6277803 | solution.py:132
  26.8 1.4 fusion.98
  32.2 1.4 fusion.98
  37.5 1.4 fusion.98
  42.9 1.4 fusion.98
  48.3 1.4 fusion.98
  53.6 1.4 fusion.98
  59.0 1.4 fusion.98
  64.3 1.4 fusion.98
  69.7 1.4 fusion.98
  75.0 1.4 fusion.98
  80.4 1.4 fusion.98
  85.8 1.4 fusion.98
  91.1 1.4 fusion.98
  96.5 1.4 fusion.98
  101.8 1.4 fusion.98
  107.2 1.4 fusion.98
  114.9 43.8 %all-gather.4 = bf16[64,1,4]{2,1,0:T(2,128)(2,1)S(1)} all-gather(bf16[1,1,4]{2,1,0:T(2,128)(2,1)S(1)} %convert_bitcast_fusion.1), channel_id=3, replica_groups=mesh['people'=2,'tm'=64,'type'=2] {'tm'}, dimensions={0}, use_global_device_ids=true | all-gather | bytes 520 | tf_op jit(solution)/shard_map/all_gather | solution.py:25
  158.7 1.6 exponential_select_fusion
  160.4 36.0 %all-gather.8.cloned.1.call-done = bf16[64,4,64,64]{3,2,1,0:T(8,128)(2,1)} async-done(((bf16[1,4,64,64]{3,2,1,0:T(8,128)(2,1)}), bf16[64,4,64,64]{3,2,1,0:T(8,128)(2,1)}) %all-gather.8.cloned.1.call-update) | async-done | bytes 2097168 | tf_op jit(solution)/shard_map/all_gather | solution.py:25
  196.4 86.0 %while.47 = (s32[]{:T(128)}, f32[1,4,64,64]{2,3,1,0:T(8,128)S(1)}, f32[1,4]{1,0:T(1,128)S(1)}, s32[]{:T(128)}, bf16[64,1,4,64,64]{4,3,2,0,1:T(8,128)(2,1)}, /*in...) while((s32[]{:T(128)}, f32[1,4,64,64]{2,3,1,0:T(8,128)S(1)}, f32[1,4]{1,0:T(1,128)S(1)}, ...), condition=%wide.region_13.14_spmd.clone, body=%wide.region_11.13_spmd.clone.sunk | while | flops 12632092 | bytes 393958 | solution.py:42
  203.1 1.2 fusion.105
  209.9 1.2 fusion.105
  282.9 438.0 %while.48 = (s32[]{:T(128)}, f32[1,4,64]{2,1,0:T(4,128)S(1)}, f32[1,4]{1,0:T(1,128)S(1)}, f32[1,4,64]{2,1,0:T(4,128)S(1)}, f32[256,1,4,64]{3,2,1,0:T(4,128)S(1)}...) while((s32[]{:T(128)}, f32[1,4,64]{2,1,0:T(4,128)S(1)}, ...), condition=%wide.region_19.20_spmd.clone, body=%wide.region_17.19_spmd.clone.sunk | while | flops 198407 | bytes 81608 | solution.py:150
  721.0 37.5 %all-gather.5 = f32[64,1,4]{2,1,0:T(1,128)S(1)} all-gather(f32[1,1,4]{2,1,0:T(1,128)S(1)} %fusion.65), channel_id=4, replica_groups=mesh['people'=2,'tm'=64,'type'=2] {'tm'}, dimensions={0}, use_global_device_ids=true | all-gather | bytes 1040 | tf_op jit(solution)/shard_map/all_gather | solution.py:157
  759.7 3.8 all-reduce
  764.1 1.3 fusion.69
  767.4 324.4 %all-reduce.1 = (f32[4,64]{1,0:T(4,128)S(1)}, f32[4]{0:T(128)S(1)}) all-reduce(f32[4,64]{1,0:T(4,128)S(1)} %bitcast_multiply_fusion.1, f32[4]{0:T(128)S(1)} %get-tuple-element.317), channel_id=1, replica_groups=mesh['people'=2,'tm'=64,'type'=2] {'people','tm'}, use_global_device_ids=true, to_apply=%region_23.24 | all-reduce | flops 260 | bytes 2080 | tf_op jit(solution)/shard_map/psum | solution.py:166
  (2287 shorter events, 591.7 us)
Async XLA Ops:
  7.2 17.2 %copy-start = (bf16[128,256]{1,0:T(8,128)(2,1)S(1)}, bf16[128,256]{1,0:T(8,128)(2,1)}, u32[]{:S(2)}) copy-start(bf16[128,256]{1,0:T(8,128)(2,1)} %param.23) | copy-start | bytes 196612
  7.2 17.0 %copy-start.1 = (bf16[3,128,128]{2,1,0:T(8,128)(2,1)S(1)}, bf16[3,128,128]{2,1,0:T(8,128)(2,1)}, u32[]{:S(2)}) copy-start(bf16[3,128,128]{2,1,0:T(8,128)(2,1)} %param.22) | copy-start | bytes 294916
  7.2 189.2 %all-gather.8.cloned.1.call-start = ((), (), s32[]{:S(2)}) async-start(), calls=%async_computation | async-start | bytes 4259840 | tf_op jit(solution)/shard_map/all_gather | solution.py:25
  8.0 11.6 %collective-permute-start = (bf16[3,1,5]{2,0,1:T(4,128)(2,1)S(1)}, bf16[3,1,5]{2,0,1:T(4,128)(2,1)S(1)}, u32[]{:S(2)}, u32[]{:S(2)}) collective-permute-start(bf16[3,1,5]{2,0,1:T(4,128)(2,1)S(1)} %get-tuple-element.343), channel_id=1, source_target_pairs={{0,2},{2,4},{4,6},{6,8},{8,10},{10,12},{12,14},{14,16},{16,18},{18... | collective-permute-start | bytes 98 | tf_op jit(solution)/shard_map/ppermute | solution.py:14
  12.6 7.0 collective-permute-start.1
  26.5 86.6 %copy-start.2 = (f32[4,64]{1,0:T(4,128)S(1)}, f32[4,64]{1,0:T(4,128)}, u32[]{:S(2)}) copy-start(f32[4,64]{1,0:T(4,128)} %param.26) | copy-start | bytes 3076
  26.5 86.7 %copy-start.5 = (u32[256]{0:T(256)S(1)}, u32[256]{0:T(256)}, u32[]{:S(2)}) copy-start(u32[256]{0:T(256)} %constant.125) | copy-start | bytes 3076
  196.4 567.1 %copy-start.4 = (f32[8]{0:T(128)S(1)}, f32[8]{0:T(128)}, u32[]{:S(2)}) copy-start(f32[8]{0:T(128)} %param.27) | copy-start | bytes 100
  767.3 325.1 %copy-start.3 = (f32[4]{0:T(128)}, f32[4]{0:T(128)S(1)}, u32[]{:S(2)}) copy-start(f32[4]{0:T(128)S(1)} %get-tuple-element.318) | copy-start | bytes 52
Sparse Core Ops, SparseCore 0:
  113.1 83.2 all-gather.7
